TPU v7x, 32 devices: a whole 2x2x4 slice. The times are simulated.
32 devices in a mesh: ctx: 4 (over y, x), dp: 4 (over z), tp: 2 (over core).
Axes of the slice: x: 2, y: 2, z: 4, core: 2. Of those that a mesh axis runs over, the one named last changes fastest.
Arguments:
- queries: bfloat16 [4, 512, 32, 128], P('dp', 'ctx', 'tp'), may hold values from -21 to 21
- keys: bfloat16 [4, 512, 4, 128], P('dp', 'ctx', 'tp'), may hold values from -6 to 6
- values: bfloat16 [4, 512, 4, 128], P('dp', 'ctx', 'tp'), may hold values from -6 to 6
- output_cotangent: bfloat16 [4, 512, 32, 128], P('dp', 'ctx', 'tp'), may hold values from -6 to 6
- features: bfloat16 [4, 512, 4096], P('dp', 'ctx'), may hold values from -60 to 60
- doc_lengths: int32 [4, 48], P('dp'), may hold values from 1 to 16, 512 in all within a row
- rope_num: int32 [64], replicated, may hold values from 1 to 40
- rope_den: int32 [64], replicated, may hold values from 1 to 8
- param: float32 [4096, 512], P('dp', 'tp'), may hold values from -0.4375 to 0.4375
- first_moment_state: float32 [4096, 512], P('dp', 'tp'), may hold values from -4 to 4
- second_moment_state: float32 [4096, 512], P('dp', 'tp'), may hold values from 0.05 to 1
Outputs:
- grad_queries: bfloat16 [4, 512, 32, 128], P('dp', 'ctx', 'tp')
- grad_keys: bfloat16 [4, 512, 4, 128], P('dp', 'ctx', 'tp')
- value_gradient: bfloat16 [4, 512, 4, 128], P('dp', 'ctx', 'tp')
- new_param: float32 [4096, 512], P('dp', 'tp')
- new_first: float32 [4096, 512], P('dp', 'tp')
- new_second: float32 [4096, 512], P('dp', 'tp')
Inputs may be any that keep to these rules, and one draw needn't show every extreme that they name: `doc_lengths`: each row's 48 lengths sum to 512, and the largest of each row is exactly 16.
All inputs are finite; a program needn't handle non-finite values.
Results may differ from a plain program's by a relative error of at most 0.0064.
Values may be sent and summed in bfloat16 or wider, within the bound.
No kernel may reach another device: no remote copies, remote signals or barrier semaphores. Data moves between devices by JAX's collectives and lax.ppermute only.
A program may use at most 64 MiB of HBM per device.

v0:
```python
from functools import reduce
import math
import jax
import jax.numpy as jnp
from jax import lax
from jax.sharding import PartitionSpec as P

ROPE_BASE = 500000.0
NEG_FILL = -1e30
CLIP_NORM = 1000.0
LEARN_RATE = 0.0001
DECAY_RATE = 0.1
BETA_ONE = 0.9
BETA_TWO = 0.95
ADAM_EPS = 1e-08
FIRST_FIX = 1.0 - 0.9**10
SECOND_FIX = 1.0 - 0.95**10


def shifted(array, axis, by):
    peers = lax.axis_size(axis)
    pairs = [(i, i + by) for i in range(peers) if 0 <= i + by < peers]
    return lax.ppermute(array, axis, pairs)


def doc_layout(lengths_row, token_index):
    doc_ends = jnp.cumsum(lengths_row)
    passed = doc_ends[None, :] <= token_index[:, None]
    doc_start = jnp.max(jnp.where(passed, doc_ends[None, :], 0), axis=1)
    doc_id = jnp.sum(passed.astype(jnp.int32), axis=1)
    return (doc_id, (token_index - doc_start).astype(jnp.float32))


def rope_tables(position, rope_num, rope_den, head_dim):
    expo = jnp.arange(head_dim // 2, dtype=jnp.float32) * (2.0 / head_dim)
    freq = (
        jnp.exp(-math.log(ROPE_BASE) * expo)
        * rope_den.astype(jnp.float32)
        / rope_num.astype(jnp.float32)
    )
    angle = position[:, None] * freq[None, :]
    cosine = jnp.concatenate([jnp.cos(angle), jnp.cos(angle)], axis=1)
    sine = jnp.concatenate([jnp.sin(angle), jnp.sin(angle)], axis=1)
    return (cosine[:, None, :], sine[:, None, :])


def rotate(vectors, cosine, sine):
    half = vectors.shape[-1] // 2
    turned = jnp.concatenate([-vectors[..., half:], vectors[..., :half]], axis=-1)
    return vectors * cosine + turned * sine


def unrotate(grads_in, cosine, sine):
    half = grads_in.shape[-1] // 2
    scaled = grads_in * sine
    turned = jnp.concatenate([scaled[..., half:], -scaled[..., :half]], axis=-1)
    return grads_in * cosine + turned


def adam_update(param, first_moment_state, second_moment_state, weight_gradient, grad_total):
    clip_factor = jnp.minimum(jnp.float32(1.0), CLIP_NORM / jnp.sqrt(grad_total))
    clipped = weight_gradient * clip_factor
    new_first = BETA_ONE * first_moment_state + (1.0 - BETA_ONE) * clipped
    new_second = BETA_TWO * second_moment_state + (1.0 - BETA_TWO) * clipped * clipped
    step_size = new_first / FIRST_FIX / (jnp.sqrt(new_second / SECOND_FIX) + ADAM_EPS)
    new_param = param - LEARN_RATE * (step_size + DECAY_RATE * param)
    return (new_param, new_first, new_second)


def local(
    queries,
    keys,
    values,
    output_cotangent,
    features,
    doc_lengths,
    rope_num,
    rope_den,
    param,
    first_moment_state,
    second_moment_state,
):
    tok_rows = queries.shape[1]
    head_count = queries.shape[2]
    head_dim = queries.shape[3]
    kv_count = keys.shape[2]
    group_size = head_count // kv_count
    n_ctx = lax.axis_size("ctx")
    place = lax.axis_index("ctx")
    seq_len = tok_rows * n_ctx
    doc_most = seq_len // 32
    reach = (doc_most + tok_rows - 2) // tok_rows
    scale = head_dim ** (-0.5)
    lengths_row = doc_lengths[0]
    own_index = place * tok_rows + jnp.arange(tok_rows, dtype=jnp.int32)
    own_doc, position = doc_layout(lengths_row, own_index)
    cosine, sine = rope_tables(position, rope_num, rope_den, head_dim)
    rotated_query_rows = rotate(queries[0].astype(jnp.float32), cosine, sine).astype(jnp.bfloat16)
    rotated_query_rows = rotated_query_rows.reshape(tok_rows, kv_count, group_size, head_dim)
    rotated_key_rows = rotate(keys[0].astype(jnp.float32), cosine, sine).astype(jnp.bfloat16)
    grad_out = output_cotangent[0].reshape(tok_rows, kv_count, group_size, head_dim)
    kv_pair = jnp.stack([rotated_key_rows, values[0]])
    pairs = [kv_pair]
    offset = 1
    kv_pair = shifted(kv_pair, "ctx", 1)
    pairs.append(kv_pair)
    masks = []
    for offset in range(reach + 1):
        key_index = (place - offset) * tok_rows + jnp.arange(tok_rows, dtype=jnp.int32)
        key_doc = doc_layout(lengths_row, key_index)[0]
        valid = (
            (key_index[None, :] >= 0)
            & (key_index[None, :] <= own_index[:, None])
            & (key_doc[None, :] == own_doc[:, None])
        )
        masks.append(valid)
    score_list = []
    for pair_in, valid_in in zip(pairs, masks):
        raw = (
            jnp.einsum(
                "qhgd,khd->hgqk", rotated_query_rows, pair_in[0], preferred_element_type=jnp.float32
            )
            * scale
        )
        score_list.append(jnp.where(valid_in, raw, NEG_FILL))
    row_top = reduce(
        jnp.maximum, [jnp.max(scores, axis=-1, keepdims=True) for scores in score_list]
    )
    weight_list = [
        jnp.where(valid_in, jnp.exp(scores - row_top), 0.0)
        for scores, valid_in in zip(score_list, masks)
    ]
    row_total = reduce(
        jnp.add, [jnp.sum(weights, axis=-1, keepdims=True) for weights in weight_list]
    )
    prob_list = [weights / row_total for weights in weight_list]
    low_list = [probs.astype(jnp.bfloat16) for probs in prob_list]
    attn_out = reduce(
        jnp.add,
        [
            jnp.einsum("hgqk,khd->qhgd", probs_low, pair_in[1], preferred_element_type=jnp.float32)
            for probs_low, pair_in in zip(low_list, pairs)
        ],
    )
    delta = jnp.einsum("qhgd,qhgd->hgq", grad_out.astype(jnp.float32), attn_out)[..., None]
    query_terms = []
    key_terms = []
    for pair_in, probs, probs_low, valid_in in zip(pairs, prob_list, low_list, masks):
        dprobs = jnp.einsum(
            "qhgd,khd->hgqk", grad_out, pair_in[1], preferred_element_type=jnp.float32
        )
        dscores = (probs * (dprobs - delta)).astype(jnp.bfloat16)
        q_part = (
            jnp.einsum("hgqk,khd->qhgd", dscores, pair_in[0], preferred_element_type=jnp.float32)
            * scale
        )
        k_part = (
            jnp.einsum(
                "hgqk,qhgd->khd", dscores, rotated_query_rows, preferred_element_type=jnp.float32
            )
            * scale
        )
        v_part = jnp.einsum(
            "hgqk,qhgd->khd", probs_low, grad_out, preferred_element_type=jnp.float32
        )
        q_part, kv_part = (q_part, jnp.stack([k_part, v_part]))
        query_terms.append(q_part)
        key_terms.append(kv_part)
    query_grad = reduce(jnp.add, query_terms)
    key_total = key_terms[reach]
    offset = 0
    key_total = (
        shifted(key_total.astype(jnp.bfloat16), "ctx", -1).astype(key_total.dtype)
        + key_terms[offset]
    )
    grad_q = unrotate(query_grad.reshape(tok_rows, head_count, head_dim), cosine, sine).astype(
        jnp.bfloat16
    )
    grad_k = unrotate(key_total[0], cosine, sine).astype(jnp.bfloat16)
    grad_v = key_total[1].astype(jnp.bfloat16)
    feats = features[0]
    width = feats.shape[1]
    value_flat = grad_v.reshape(tok_rows, kv_count * head_dim)
    own_rows = param.shape[0]
    n_dp = lax.axis_size("dp")
    piece_rows = own_rows // n_ctx
    permuted = (
        feats.reshape(tok_rows, n_dp, n_ctx, piece_rows)
        .transpose(0, 2, 1, 3)
        .reshape(tok_rows, width)
    )
    pieces = lax.psum_scatter(
        lax.dot_general(
            permuted, value_flat, (((0,), (0,)), ((), ())), preferred_element_type=jnp.float32
        ),
        ("ctx", "dp"),
        scatter_dimension=0,
        tiled=True,
    )
    weight_gradient = lax.all_gather(pieces, "ctx", axis=0, tiled=True)
    norm_part = jnp.sum(weight_gradient * weight_gradient)
    grad_total = lax.psum(norm_part, ("dp", "tp"))
    new_param, new_first, new_second = adam_update(
        param, first_moment_state, second_moment_state, weight_gradient, grad_total
    )
    return (grad_q[None], grad_k[None], grad_v[None], new_param, new_first, new_second)


def solution(mesh):
    placed = (
        P("dp", "ctx", "tp", None),
        P("dp", "ctx", "tp", None),
        P("dp", "ctx", "tp", None),
        P("dp", "ctx", "tp", None),
        P("dp", "ctx", None),
        P("dp", None),
        P(),
        P(),
        P("dp", "tp"),
        P("dp", "tp"),
        P("dp", "tp"),
    )
    return jax.shard_map(
        local,
        mesh=mesh,
        in_specs=placed,
        out_specs=(
            P("dp", "ctx", "tp", None),
            P("dp", "ctx", "tp", None),
            P("dp", "ctx", "tp", None),
            P("dp", "tp"),
            P("dp", "tp"),
            P("dp", "tp"),
        ),
        check_vma=False,
    )
```

profile of v0, /device:TPU:0, one launch (start us, length us, event | category | flops | bytes accessed | tf_op | source)
XLA Modules:
  0.0 216.5 jit_solution(16039566260402643105)
XLA Ops:
  7.2 0.7 copy.135
  8.0 0.1 reduce.1
  8.2 0.1 fusion.44
  8.3 0.7 convert_divide_fusion
  9.0 0.3 multiply_cosine_fusion
  9.4 0.9 convert_bitcast_fusion.2
  10.3 0.7 fusion.45
  11.0 0.8 copy.142
  11.9 0.9 fusion.35
  12.8 0.7 pad_maximum_fusion
  13.5 5.5 %collective-permute-start = (bf16[2,128,2,128]{3,1,2,0:T(8,128)(2,1)}, bf16[2,128,2,128]{3,1,2,0:T(8,128)(2,1)}, u32[]{:S(2)}, u32[]{:S(2)}) collective-permute-start(bf16[2,128,2,128]{3,1,2,0:T(8,128)(2,1)} %pad_maximum_fusion), channel_id=1, source_target_pairs={{0,8},{8,16},{16,24},{1,9},{9,17},{17,25},{2,10},{10,18},{18,26},{... | collective-permute-start | bytes 393224 | tf_op jit(solution)/shard_map/ppermute | solution.py:23
  19.0 0.6 broadcast_compare_fusion
  19.7 0.7 copy.140
  20.4 1.2 convert_bitcast_fusion.1
  21.6 1.3 fusion.22
  22.9 2.4 %copy.138 = f32[128,2,8,64]{0,3,2,1:T(8,128)} copy(f32[128,2,8,64]{3,2,1,0:T(8,128)} %get-tuple-element.40) | data formatting | bytes 1048576 | tf_op jit(solution)/shard_map/concatenate | solution.py:49
  25.3 1.2 copy.139
  26.5 0.4 copy.137
  27.0 1.0 fusion.40
  28.0 0.8 compare_and_fusion
  28.8 1.4 fusion.24
  30.2 0.3 fusion.51
  30.5 1.2 copy.164
  31.8 1.6 copy.168
  33.4 1.0 copy.169
  34.4 1.1 fusion.52
  35.6 0.4 fusion.29
  36.0 1.0 fusion.18
  37.0 1.0 convolution_bitcast_fusion.5
  38.0 0.4 convolution_bitcast_fusion.3
  38.5 1.2 fusion.3
  39.7 0.8 multiply_reduce_fusion
  40.5 1.4 fusion.12
  42.0 1.6 fusion.11
  43.6 0.3 fusion.19
  43.9 1.3 collective-permute-start.1
  45.2 0.3 fusion.15
  45.6 5.2 %collective-permute-done.1 = bf16[2,128,2,128]{3,1,2,0:T(8,128)(2,1)S(1)} collective-permute-done((bf16[2,128,2,128]{3,1,2,0:T(8,128)(2,1)S(1)}, bf16[2,128,2,128]{3,1,2,0:T(8,128)(2,1)S(1)}, u32[]{:S(2)}, u32[]{:S(2)}) %collective-permute-start.1) | collective-permute-done | bytes 131104 | tf_op jit(solution)/shard_map/ppermute | solution.py:23
  50.9 0.1 copy.167
  51.0 0.5 copy-done.8
  51.5 2.6 %convolution_bitcast_fusion = f32[4096,256]{0,1:T(8,128)} fusion(bf16[128,256]{0,1:T(8,128)(2,1)S(1)} %bitcast.172, bf16[128,4096]{0,1:T(8,128)(2,1)S(1)} %bitcast.170), kind=kOutput, calls=%fused_computation | convolution fusion | flops 268435456 | bytes 5308416 | tf_op jit(solution)/shard_map/dot_general | solution.py:193
  54.2 0.2 all-gather.2.cloned.1.call-start
  54.4 1.0 copy-done.6
  55.4 1.3 copy.166
  56.7 1.3 copy.170
  58.0 2.5 %copy.172 = f32[1024,256]{0,1:T(8,128)} copy(f32[1024,256]{1,0:T(8,128)} %param.19) | data formatting | bytes 2097152 | tf_op args[8]
  60.5 1.2 fusion.53
  61.7 90.6 %reduce-scatter.2.cloned.1.call-done = f32[256,256]{0,1:T(8,128)} async-done(((f32[4096,256]{0,1:T(8,128)}), f32[256,256]{0,1:T(8,128)}) %reduce-scatter.2.cloned.1.call-update) | async-done | bytes 262160 | tf_op jit(solution)/shard_map/reduce_scatter | solution.py:192
  152.3 1.2 fusion.6
  153.5 0.5 copy.157
  154.0 0.5 copy.156
  154.5 0.1 broadcast_multiply_fusion
  154.7 0.3 slice_bitcast_fusion
  155.0 1.2 fusion.25
  156.2 0.7 copy.174
  157.0 0.1 fusion.39
  157.1 22.0 %all-gather.2.cloned.1.call-done = f32[1024,256]{0,1:T(8,128)} async-done(((f32[256,256]{0,1:T(8,128)}), f32[1024,256]{0,1:T(8,128)}) %all-gather.2.cloned.1.call-update) | async-done | bytes 1048592 | tf_op jit(solution)/shard_map/all_gather | solution.py:200
  179.1 2.2 %multiply_reduce_fusion.1 = f32[]{:T(128)} fusion(f32[1024,256]{0,1:T(8,128)} %all-gather.2.cloned.1.call-done), kind=kLoop, calls=%fused_computation.50 | loop fusion | flops 524287 | bytes 1048580 | tf_op jit(solution)/shard_map/reduce_sum | solution.py:201
  181.3 0.7 copy.173
  182.0 16.9 %psum.7 = f32[]{:T(128)} all-reduce(f32[]{:T(128)} %multiply_reduce_fusion.1), channel_id=1, replica_groups=mesh['ctx'=4,'dp'=4,'tp'=2] {'dp','tp'}, use_global_device_ids=true, to_apply=%region_10.11 | all-reduce | flops 1 | bytes 8 | tf_op jit(solution)/shard_map/psum | solution.py:202
  199.7 3.7 %multiply_subtract_fusion = (f32[1024,256]{0,1:T(8,128)}, f32[1024,256]{0,1:T(8,128)}, f32[1024,256]{0,1:T(8,128)S(1)}) fusion(f32[1024,256]{0,1:T(8,128)} %copy.172, f32[1024,256]{0,1:T(8,128)} %all-gather.2.cloned.1.call-done, f32[]{:T(128)S(6)} %min_shard_map.3, f32[1024,256]{0,1:T(8,128)S(1)} %copy-done.1, f32[1024,256]{0,1:T(8,128)S(1)} %copy-done.2), kind=kLoop, calls=%fused_computation.48 | loop fusion | flops 4194304 | bytes 7340036 | tf_op jit(solution)/shard_map/sub | solution.py:66
  203.3 2.5 %copy.175 = f32[1024,256]{1,0:T(8,128)} copy(f32[1024,256]{0,1:T(8,128)} %get-tuple-element.35) | data formatting | bytes 2097152
  205.9 2.5 %copy.176 = f32[1024,256]{1,0:T(8,128)} copy(f32[1024,256]{0,1:T(8,128)} %get-tuple-element.36) | data formatting | bytes 2097152
  208.4 1.3 copy.177
  (48 shorter events, 0.7 us)
Async XLA Ops:
  7.2 145.1 %reduce-scatter.2.cloned.1.call-start = ((), (), s32[]{:S(2)}) async-start(), calls=%async_computation.1 | async-start | bytes 4456448 | tf_op jit(solution)/shard_map/reduce_scatter | solution.py:192
  13.5 21.0 %collective-permute-start = (bf16[2,128,2,128]{3,1,2,0:T(8,128)(2,1)}, bf16[2,128,2,128]{3,1,2,0:T(8,128)(2,1)}, u32[]{:S(2)}, u32[]{:S(2)}) collective-permute-start(bf16[2,128,2,128]{3,1,2,0:T(8,128)(2,1)} %pad_maximum_fusion), channel_id=1, source_target_pairs={{0,8},{8,16},{16,24},{1,9},{9,17},{17,25},{2,10},{10,18},{18,26},{... | collective-permute-start | bytes 393224 | tf_op jit(solution)/shard_map/ppermute | solution.py:23
  21.6 5.4 %copy-start.11 = (bf16[1,128,2,128]{3,2,1,0:T(2,128)(2,1)S(1)}, bf16[1,128,2,128]{3,2,1,0:T(2,128)(2,1)}, u32[]{:S(2)}) copy-start(bf16[1,128,2,128]{3,2,1,0:T(2,128)(2,1)} %param.12) | copy-start | bytes 196612
  25.3 5.2 %copy-start.3 = (bf16[1,128,16,128]{3,2,1,0:T(8,128)(2,1)S(1)}, bf16[1,128,16,128]{3,2,1,0:T(8,128)(2,1)}, u32[]{:S(2)}) copy-start(bf16[1,128,16,128]{3,2,1,0:T(8,128)(2,1)} %param.14) | copy-start | bytes 1572868
  28.0 2.5 %copy-start.10 = (bf16[128,2,128,1]{2,0,3,1:T(8,128)(2,1)}, bf16[128,2,128,1]{2,0,3,1:T(8,128)(2,1)S(1)}, u32[]{:S(2)}) copy-start(bf16[128,2,128,1]{2,0,3,1:T(8,128)(2,1)S(1)} %fusion.40) | copy-start | bytes 196612
  33.4 2.6 %copy-start.12 = (bf16[128,2,8,128]{0,3,2,1:T(8,128)(2,1)S(1)}, bf16[128,2,8,128]{0,3,2,1:T(8,128)(2,1)}, u32[]{:S(2)}) copy-start(bf16[128,2,8,128]{0,3,2,1:T(8,128)(2,1)} %copy.164) | copy-start | bytes 1572868
  36.0 2.0 copy-start.14
  42.0 1.9 copy-start.15
  42.0 8.8 %copy-start.13 = (f32[1,128,2,128]{3,1,2,0:T(8,128)S(1)}, f32[1,128,2,128]{3,1,2,0:T(8,128)}, u32[]{:S(2)}) copy-start(f32[1,128,2,128]{3,1,2,0:T(8,128)} %convolution_bitcast_fusion.5) | copy-start | bytes 393220
  42.0 9.5 %copy-start = (bf16[128,4,4,256]{0,3,2,1:T(8,128)(2,1)S(1)}, bf16[128,4,4,256]{0,3,2,1:T(8,128)(2,1)}, u32[]{:S(2)}) copy-start(bf16[128,4,4,256]{0,3,2,1:T(8,128)(2,1)} %copy.169) | copy-start | bytes 3145732
  43.6 2.0 copy-start.4
  43.9 6.9 %collective-permute-start.1 = (bf16[2,128,2,128]{3,1,2,0:T(8,128)(2,1)S(1)}, bf16[2,128,2,128]{3,1,2,0:T(8,128)(2,1)S(1)}, u32[]{:S(2)}, u32[]{:S(2)}) collective-permute-start(bf16[2,128,2,128]{3,1,2,0:T(8,128)(2,1)S(1)} %pad_maximum_fusion.1), channel_id=1, source_target_pairs={{8,0},{16,8},{24,16},{9,1},{17,9},{25,17},{10,2},{18,10},{26,18},{... | collective-permute-start | bytes 393224 | tf_op jit(solution)/shard_map/ppermute | solution.py:23
  50.9 0.6 copy-start.8
  54.1 1.2 copy-start.6
  54.1 2.5 %copy-start.7 = (f32[1024,256]{1,0:T(8,128)S(1)}, f32[1024,256]{1,0:T(8,128)}, u32[]{:S(2)}) copy-start(f32[1024,256]{1,0:T(8,128)} %param.21) | copy-start | bytes 3145732
  54.2 98.2 %copy-start.5 = (bf16[2,8,128,128]{2,3,1,0:T(8,128)(2,1)S(1)}, bf16[2,8,128,128]{2,3,1,0:T(8,128)(2,1)}, u32[]{:S(2)}) copy-start(bf16[2,8,128,128]{2,3,1,0:T(8,128)(2,1)} %copy-done.4) | copy-start | bytes 1572868
  54.2 125.0 %all-gather.2.cloned.1.call-start = ((), (), s32[]{:S(2)}) async-start(), calls=%async_computation.2 | async-start | bytes 1310720 | tf_op jit(solution)/shard_map/all_gather | solution.py:200
  154.7 1.6 copy-start.9
  155.0 44.6 %copy-start.1 = (f32[1024,256]{0,1:T(8,128)S(1)}, f32[1024,256]{0,1:T(8,128)}, u32[]{:S(2)}) copy-start(f32[1024,256]{0,1:T(8,128)} %copy.166) | copy-start | bytes 3145732
  155.0 44.6 %copy-start.2 = (f32[1024,256]{0,1:T(8,128)S(1)}, f32[1024,256]{0,1:T(8,128)}, u32[]{:S(2)}) copy-start(f32[1024,256]{0,1:T(8,128)} %copy.170) | copy-start | bytes 3145732
Sparse Core Ops, SparseCore 0:
  54.3 97.9 reduce-scatter.1
  154.1 24.9 all-gather.1
where the time goes:
time: 218 us; the launch traced here: 217 us
  waiting for transfers between devices  118 us (54%)
  local copies, waits for them, and re-layouts  26 us (12%)
  other arithmetic  19.8 us (9%)
  blocking collectives  16.9 us (8%)
  between operations  15.2 us (7%)
  matrix products  13.7 us (6%)
  starting transfers between devices  7.07 us (3%)
    reduce_scatter x1, waiting for transfers between devices, local(): lax.psum_scatter(lax.dot_general(permuted, value_flat, (((0,), (0,)), (()...  90.6 us
    all_gather x1, waiting for transfers between devices, local(): weight_gradient = lax.all_gather(pieces, 'ctx', axis=0, tiled=True)  22 us
    unnamed x42, local copies, waits for them, and re-layouts  16.9 us
    psum x1, blocking collectives, local(): grad_total = lax.psum(norm_part, ('dp', 'tp'))  16.9 us
    ppermute x2, starting transfers between devices, shifted(): return lax.ppermute(array, axis, pairs)  6.81 us
    ppermute x2, waiting for transfers between devices, shifted(): return lax.ppermute(array, axis, pairs)  5.25 us
  transfers between devices with their start and end apart: 4, of which 3 were waited for; matrix products, arithmetic and copies ran while one was open for 12% of the time, Pallas kernels for 0%

commit v1 on v0

--- a/solution.py
+++ b/solution.py
@@ -197,7 +197,16 @@
         scatter_dimension=0,
         tiled=True,
     )
-    weight_gradient = lax.all_gather(pieces, "ctx", axis=0, tiled=True)
+    ways = lax.axis_size("ctx")
+    up = [(d, (d + 1) % ways) for d in range(ways)]
+    down = [(d, (d - 1) % ways) for d in range(ways)]
+    earlier, later = ([pieces], [pieces])
+    for _ in range(ways // 2):
+        earlier.append(lax.ppermute(earlier[-1], "ctx", up))
+    for _ in range((ways - 1) // 2):
+        later.append(lax.ppermute(later[-1], "ctx", down))
+    line = jnp.concatenate([*earlier[::-1], *later[1:]], axis=0)
+    weight_gradient = jnp.roll(line, (lax.axis_index("ctx") - ways // 2) * pieces.shape[0], axis=0)
     norm_part = jnp.sum(weight_gradient * weight_gradient)
     grad_total = lax.psum(norm_part, ("dp", "tp"))
     new_param, new_first, new_second = adam_update(

time: 218 us -> 201 us (0.922)
  waiting for transfers between devices: 118 us -> 107 us
  other arithmetic: 19.8 us -> 16.9 us
  starting transfers between devices: 7.07 us -> 9.96 us
  blocking collectives: 16.9 us -> 14.3 us
    all_gather x1 -> x0, waiting for transfers between devices: 22 us -> none  [local(): weight_gradient = lax.all_gather(pieces, 'ctx', axis=0, tiled=True)]
    ppermute x0 -> x3, waiting for transfers between devices: none -> 12.7 us  [the longest x2 10.8 us: local(): earlier.append(lax.ppermute(earlier[-1], 'ctx', up))]
    ppermute x0 -> x3, starting transfers between devices: none -> 2.98 us  [the longest x1 2.97 us: local(): later.append(lax.ppermute(later[-1], 'ctx', down))]
    psum x1, blocking collectives: 16.9 us -> 14.3 us  [local(): grad_total = lax.psum(norm_part, ('dp', 'tp'))]
    unnamed x42 -> x65, local copies, waits for them, and re-layouts: 16.9 us -> 17.1 us
  transfers between devices with their start and end apart: 4 -> 6, of which waited for: 3 -> 5; matrix products, arithmetic and copies ran while one was open for 12% -> 11% of each run, Pallas kernels for 0% -> 0%
where the time goes in v1:
time: 201 us; the launch traced here: 200 us
  waiting for transfers between devices  107 us (53%)
  local copies, waits for them, and re-layouts  24.7 us (12%)
  other arithmetic  16.9 us (8%)
  between operations  15.4 us (8%)
  blocking collectives  14.3 us (7%)
  matrix products  12.7 us (6%)
  starting transfers between devices  9.96 us (5%)
    reduce_scatter x1, waiting for transfers between devices, local(): lax.psum_scatter(lax.dot_general(permuted, value_flat, (((0,), (0,)), (()...  88.6 us
    unnamed x65, local copies, waits for them, and re-layouts  17.1 us
    psum x1, blocking collectives, local(): grad_total = lax.psum(norm_part, ('dp', 'tp'))  14.3 us
    ppermute x2, waiting for transfers between devices, local(): earlier.append(lax.ppermute(earlier[-1], 'ctx', up))  10.8 us
    ppermute x2, starting transfers between devices, shifted(): return lax.ppermute(array, axis, pairs)  6.95 us
    ppermute x2, waiting for transfers between devices, shifted(): return lax.ppermute(array, axis, pairs)  5.25 us
  transfers between devices with their start and end apart: 6, of which 5 were waited for; matrix products, arithmetic and copies ran while one was open for 11% of the time, Pallas kernels for 0%

profile of v1, /device:TPU:0, one launch (start us, length us, event | category | flops | bytes accessed | tf_op | source)
XLA Modules:
  0.0 200.5 jit_solution(3920284846306875344)
XLA Ops:
  7.2 0.8 copy.135
  8.1 0.1 reduce.1
  8.3 0.7 convert_divide_fusion
  9.0 0.3 multiply_cosine_fusion
  9.5 0.9 convert_bitcast_fusion.2
  10.4 0.7 fusion.45
  11.1 0.8 copy.142
  11.9 0.9 fusion.35
  12.9 0.7 pad_maximum_fusion
  13.5 5.5 %collective-permute-start = (bf16[2,128,2,128]{3,1,2,0:T(8,128)(2,1)}, bf16[2,128,2,128]{3,1,2,0:T(8,128)(2,1)}, u32[]{:S(2)}, u32[]{:S(2)}) collective-permute-start(bf16[2,128,2,128]{3,1,2,0:T(8,128)(2,1)} %pad_maximum_fusion), channel_id=1, source_target_pairs={{0,8},{8,16},{16,24},{1,9},{9,17},{17,25},{2,10},{10,18},{18,26},{... | collective-permute-start | bytes 393224 | tf_op jit(solution)/shard_map/ppermute | solution.py:23
  19.1 0.5 broadcast_compare_fusion
  19.7 0.7 copy.140
  20.4 0.1 convert_bitcast_fusion.1
  20.6 1.3 fusion.22
  21.9 1.6 copy.138
  23.5 0.4 copy.139
  23.9 0.4 copy.137
  24.4 1.0 fusion.40
  25.4 0.9 compare_and_fusion
  26.3 1.1 fusion.24
  27.3 0.3 fusion.51
  27.6 1.2 copy.164
  28.9 1.6 copy.168
  30.5 1.0 copy.169
  31.5 1.2 fusion.52
  32.8 0.4 fusion.29
  33.2 1.0 fusion.18
  34.2 1.0 convolution_bitcast_fusion.5
  35.2 0.4 convolution_bitcast_fusion.3
  35.6 1.2 fusion.3
  36.8 0.8 multiply_reduce_fusion
  37.7 1.5 fusion.12
  39.2 1.3 fusion.11
  40.5 0.3 fusion.19
  40.9 1.4 collective-permute-start.1
  42.3 0.3 fusion.15
  42.6 5.2 %collective-permute-done.1 = bf16[2,128,2,128]{3,1,2,0:T(8,128)(2,1)S(1)} collective-permute-done((bf16[2,128,2,128]{3,1,2,0:T(8,128)(2,1)S(1)}, bf16[2,128,2,128]{3,1,2,0:T(8,128)(2,1)S(1)}, u32[]{:S(2)}, u32[]{:S(2)}) %collective-permute-start.1) | collective-permute-done | bytes 131104 | tf_op jit(solution)/shard_map/ppermute | solution.py:23
  47.9 0.1 copy.167
  48.1 2.6 %convolution_bitcast_fusion = f32[4096,256]{0,1:T(8,128)} fusion(bf16[128,256]{0,1:T(8,128)(2,1)S(1)} %bitcast.172, bf16[128,4096]{0,1:T(8,128)(2,1)S(1)} %bitcast.170), kind=kOutput, calls=%fused_computation | convolution fusion | flops 268435456 | bytes 5308416 | tf_op jit(solution)/shard_map/dot_general | solution.py:193
  50.8 1.2 copy-done.10
  51.9 1.3 copy.166
  53.3 1.3 copy.170
  54.6 2.6 %copy.172 = f32[1024,256]{0,1:T(8,128)} copy(f32[1024,256]{1,0:T(8,128)} %param.19) | data formatting | bytes 2097152 | tf_op args[8]
  57.2 0.3 fusion.53
  57.5 1.2 fusion.6
  58.7 0.5 copy.157
  59.2 0.5 copy.156
  59.7 0.1 broadcast_multiply_fusion
  59.8 0.3 slice_bitcast_fusion
  60.2 88.6 %reduce-scatter.2.cloned.1.call-done = f32[256,256]{0,1:T(8,128)} async-done(((f32[4096,256]{0,1:T(8,128)}), f32[256,256]{0,1:T(8,128)}) %reduce-scatter.2.cloned.1.call-update) | async-done | bytes 262160 | tf_op jit(solution)/shard_map/reduce_scatter | solution.py:192
  148.8 1.1 fusion.25
  149.9 6.6 %collective-permute-done.2 = f32[256,256]{0,1:T(8,128)S(1)} collective-permute-done((f32[256,256]{0,1:T(8,128)}, f32[256,256]{0,1:T(8,128)S(1)}, u32[]{:S(2)}, u32[]{:S(2)}) %collective-permute-start.2) | collective-permute-done | bytes 262176 | tf_op jit(solution)/shard_map/ppermute | solution.py:205
  156.6 0.7 copy.174
  157.4 3.0 %collective-permute-start.4 = (f32[256,256]{0,1:T(8,128)S(1)}, f32[256,256]{0,1:T(8,128)S(1)}, u32[]{:S(2)}, u32[]{:S(2)}) collective-permute-start(f32[256,256]{0,1:T(8,128)S(1)} %copy-done.12), channel_id=1, source_target_pairs={{0,24},{8,0},{16,8},{24,16},{1,25},{9,1},{17,9},{25,17},{2,26},{10... | collective-permute-start | bytes 786440 | tf_op jit(solution)/shard_map/ppermute | solution.py:207
  160.4 4.3 %collective-permute-done.3 = f32[256,256]{0,1:T(8,128)S(1)} collective-permute-done((f32[256,256]{0,1:T(8,128)S(1)}, f32[256,256]{0,1:T(8,128)S(1)}, u32[]{:S(2)}, u32[]{:S(2)}) %collective-permute-start.3) | collective-permute-done | bytes 262176 | tf_op jit(solution)/shard_map/ppermute | solution.py:205
  164.8 1.9 collective-permute-done.4
  166.9 1.3 copy-done.6
  168.2 0.9 multiply_reduce_fusion.1
  169.1 0.7 copy.173
  169.8 14.3 %psum.7 = f32[]{:T(128)} all-reduce(f32[]{:T(128)} %multiply_reduce_fusion.1), channel_id=1, replica_groups=mesh['ctx'=4,'dp'=4,'tp'=2] {'dp','tp'}, use_global_device_ids=true, to_apply=%region_10.11 | all-reduce | flops 1 | bytes 8 | tf_op jit(solution)/shard_map/psum | solution.py:211
  184.9 3.5 %multiply_subtract_fusion = (f32[1024,256]{0,1:T(8,128)}, f32[1024,256]{0,1:T(8,128)}, f32[1024,256]{0,1:T(8,128)}) fusion(f32[1024,256]{0,1:T(8,128)S(1)} %copy-done.2, f32[]{:T(128)S(6)} %min_shard_map.3, f32[2048,256]{0,1:T(8,128)} %copy-done.6, s32[]{:T(128)S(6)} %select_n.36, f32[1024,256]{0,1:T(8,128)S(1)} %copy-done, f32[1024,256]{0,1:T(8,128)S(1)} %copy-done.1), kind=kLoop, calls=%fused_computation.48 | loop fusion | flops 4194304 | bytes 7340040 | tf_op jit(solution)/shard_map/sub | solution.py:66
  188.3 2.7 %copy.175 = f32[1024,256]{1,0:T(8,128)} copy(f32[1024,256]{0,1:T(8,128)} %get-tuple-element.35) | data formatting | bytes 2097152
  191.0 1.3 copy.176
  192.3 1.3 copy.177
  (75 shorter events, 1.1 us)
Async XLA Ops:
  7.2 13.2 %copy-start.18 = (bf16[1,128,16,128]{3,2,1,0:T(8,128)(2,1)S(1)}, bf16[1,128,16,128]{3,2,1,0:T(8,128)(2,1)}, u32[]{:S(2)}) copy-start(bf16[1,128,16,128]{3,2,1,0:T(8,128)(2,1)} %param.11) | copy-start | bytes 1572868
  7.2 141.6 %reduce-scatter.2.cloned.1.call-start = ((), (), s32[]{:S(2)}) async-start(), calls=%async_computation.1 | async-start | bytes 4456448 | tf_op jit(solution)/shard_map/reduce_scatter | solution.py:192
  13.5 18.0 %collective-permute-start = (bf16[2,128,2,128]{3,1,2,0:T(8,128)(2,1)}, bf16[2,128,2,128]{3,1,2,0:T(8,128)(2,1)}, u32[]{:S(2)}, u32[]{:S(2)}) collective-permute-start(bf16[2,128,2,128]{3,1,2,0:T(8,128)(2,1)} %pad_maximum_fusion), channel_id=1, source_target_pairs={{0,8},{8,16},{16,24},{1,9},{9,17},{17,25},{2,10},{10,18},{18,26},{... | collective-permute-start | bytes 393224 | tf_op jit(solution)/shard_map/ppermute | solution.py:23
  23.5 0.9 copy-start.17
  25.4 2.3 %copy-start.15 = (bf16[128,2,128,1]{2,0,3,1:T(8,128)(2,1)}, bf16[128,2,128,1]{2,0,3,1:T(8,128)(2,1)S(1)}, u32[]{:S(2)}) copy-start(bf16[128,2,128,1]{2,0,3,1:T(8,128)(2,1)S(1)} %fusion.40) | copy-start | bytes 196612
  26.2 1.4 copy-start.7
  31.5 1.6 copy-start.19
  34.2 1.0 copy-start.22
  37.7 1.5 copy-start.20
  39.2 1.6 copy-start.23
  40.5 2.1 %copy-start.8 = (bf16[2,8,128,128]{2,3,1,0:T(8,128)(2,1)}, bf16[2,8,128,128]{2,3,1,0:T(8,128)(2,1)S(1)}, u32[]{:S(2)}) copy-start(bf16[2,8,128,128]{2,3,1,0:T(8,128)(2,1)S(1)} %fusion.11) | copy-start | bytes 1572868
  40.5 7.4 %copy-start.21 = (f32[1,128,2,128]{3,1,2,0:T(8,128)S(1)}, f32[1,128,2,128]{3,1,2,0:T(8,128)}, u32[]{:S(2)}) copy-start(f32[1,128,2,128]{3,1,2,0:T(8,128)} %convolution_bitcast_fusion.5) | copy-start | bytes 393220
  40.5 7.5 %copy-start.3 = (bf16[128,4,4,256]{0,3,2,1:T(8,128)(2,1)S(1)}, bf16[128,4,4,256]{0,3,2,1:T(8,128)(2,1)}, u32[]{:S(2)}) copy-start(bf16[128,4,4,256]{0,3,2,1:T(8,128)(2,1)} %copy.169) | copy-start | bytes 3145732
  40.9 7.0 %collective-permute-start.1 = (bf16[2,128,2,128]{3,1,2,0:T(8,128)(2,1)S(1)}, bf16[2,128,2,128]{3,1,2,0:T(8,128)(2,1)S(1)}, u32[]{:S(2)}, u32[]{:S(2)}) collective-permute-start(bf16[2,128,2,128]{3,1,2,0:T(8,128)(2,1)S(1)} %pad_maximum_fusion.1), channel_id=1, source_target_pairs={{8,0},{16,8},{24,16},{9,1},{17,9},{25,17},{10,2},{18,10},{26,18},{... | collective-permute-start | bytes 393224 | tf_op jit(solution)/shard_map/ppermute | solution.py:23
  47.9 2.8 %copy-start.13 = (bf16[1,128,2,128]{3,1,2,0:T(8,128)(2,1)}, bf16[1,128,2,128]{3,1,2,0:T(8,128)(2,1)S(1)}, u32[]{:S(2)}) copy-start(bf16[1,128,2,128]{3,1,2,0:T(8,128)(2,1)S(1)} %slice.88) | copy-start | bytes 196612
  50.7 1.2 copy-start.10
  50.7 2.5 %copy-start.11 = (f32[1024,256]{1,0:T(8,128)S(1)}, f32[1024,256]{1,0:T(8,128)}, u32[]{:S(2)}) copy-start(f32[1024,256]{1,0:T(8,128)} %param.21) | copy-start | bytes 3145732
  53.3 3.9 %copy-start.16 = (bf16[128,2,128,1]{2,0,3,1:T(8,128)(2,1)S(1)}, bf16[128,2,128,1]{2,0,3,1:T(8,128)(2,1)}, u32[]{:S(2)}) copy-start(bf16[128,2,128,1]{2,0,3,1:T(8,128)(2,1)} %copy-done.15) | copy-start | bytes 196612
  54.6 2.9 %copy-start.9 = (bf16[2,8,128,128]{2,3,1,0:T(8,128)(2,1)S(1)}, bf16[2,8,128,128]{2,3,1,0:T(8,128)(2,1)}, u32[]{:S(2)}) copy-start(bf16[2,8,128,128]{2,3,1,0:T(8,128)(2,1)} %copy-done.8) | copy-start | bytes 1572868
  148.8 7.7 %collective-permute-start.2 = (f32[256,256]{0,1:T(8,128)}, f32[256,256]{0,1:T(8,128)S(1)}, u32[]{:S(2)}, u32[]{:S(2)}) collective-permute-start(f32[256,256]{0,1:T(8,128)} %reduce-scatter.2.cloned.1.call-done), channel_id=1, source_target_pairs={{0,8},{8,16},{16,24},{24,0},{1,9},{9,17},{17,25},{25,1},{2,10},{10... | collective-permute-start | bytes 786440 | tf_op jit(solution)/shard_map/ppermute | solution.py:205
  148.8 7.8 %copy-start.14 = (bf16[1,128,2,128]{3,1,2,0:T(8,128)(2,1)S(1)}, bf16[1,128,2,128]{3,1,2,0:T(8,128)(2,1)}, u32[]{:S(2)}) copy-start(bf16[1,128,2,128]{3,1,2,0:T(8,128)(2,1)} %copy-done.13) | copy-start | bytes 196612
  148.8 8.7 %copy-start.12 = (f32[256,256]{0,1:T(8,128)S(1)}, f32[256,256]{0,1:T(8,128)}, u32[]{:S(2)}) copy-start(f32[256,256]{0,1:T(8,128)} %reduce-scatter.2.cloned.1.call-done) | copy-start | bytes 786436
  156.5 8.2 %collective-permute-start.3 = (f32[256,256]{0,1:T(8,128)S(1)}, f32[256,256]{0,1:T(8,128)S(1)}, u32[]{:S(2)}, u32[]{:S(2)}) collective-permute-start(f32[256,256]{0,1:T(8,128)S(1)} %collective-permute-done.2), channel_id=1, source_target_pairs={{0,8},{8,16},{16,24},{24,0},{1,9},{9,17},{17,25},{25,1},{2,10},{10... | collective-permute-start | bytes 786440 | tf_op jit(solution)/shard_map/ppermute | solution.py:205
  157.4 9.2 %collective-permute-start.4 = (f32[256,256]{0,1:T(8,128)S(1)}, f32[256,256]{0,1:T(8,128)S(1)}, u32[]{:S(2)}, u32[]{:S(2)}) collective-permute-start(f32[256,256]{0,1:T(8,128)S(1)} %copy-done.12), channel_id=1, source_target_pairs={{0,24},{8,0},{16,8},{24,16},{1,25},{9,1},{17,9},{25,17},{2,26},{10... | collective-permute-start | bytes 786440 | tf_op jit(solution)/shard_map/ppermute | solution.py:207
  164.7 20.1 %copy-start = (f32[1024,256]{0,1:T(8,128)S(1)}, f32[1024,256]{0,1:T(8,128)}, u32[]{:S(2)}) copy-start(f32[1024,256]{0,1:T(8,128)} %copy.166) | copy-start | bytes 3145732
  164.8 20.1 %copy-start.1 = (f32[1024,256]{0,1:T(8,128)S(1)}, f32[1024,256]{0,1:T(8,128)}, u32[]{:S(2)}) copy-start(f32[1024,256]{0,1:T(8,128)} %copy.170) | copy-start | bytes 3145732
  164.8 20.1 %copy-start.2 = (f32[1024,256]{0,1:T(8,128)S(1)}, f32[1024,256]{0,1:T(8,128)}, u32[]{:S(2)}) copy-start(f32[1024,256]{0,1:T(8,128)} %copy.172) | copy-start | bytes 3145732
  166.8 1.4 copy-start.6
  188.3 2.7 %copy-start.5 = (f32[1024,256]{0,1:T(8,128)S(1)}, f32[1024,256]{0,1:T(8,128)}, u32[]{:S(2)}) copy-start(f32[1024,256]{0,1:T(8,128)} %get-tuple-element.36) | copy-start | bytes 3145732
  188.3 4.0 %copy-start.4 = (f32[1024,256]{0,1:T(8,128)S(1)}, f32[1024,256]{0,1:T(8,128)}, u32[]{:S(2)}) copy-start(f32[1024,256]{0,1:T(8,128)} %get-tuple-element.37) | copy-start | bytes 3145732
Sparse Core Ops, SparseCore 0:
  50.9 97.8 reduce-scatter.1
